TPU v7x, 32 devices: a whole 2x2x4 slice. The times are simulated.
32 devices in a mesh: group: 2 (over x), strip: 16 (over z, y, core).
Axes of the slice: x: 2, y: 2, z: 4, core: 2. Of those that a mesh axis runs over, the one named last changes fastest.
Arguments:
- strip_fields: float32 [3, 64, 128, 128], P(None, ('group', 'strip')), may hold values from -18 to 18
- strip_riser: int32 [64, 1], P('group'), may hold values from 0 to 3; in each aligned block of 2 rows (0 to 1, 2 to 3, ...) at most 2 rows name the same one
- strip_node: int32 [64], P('group'), may hold values from 0 to 1023
- riser_owner: int32 [2, 4], P('group'), may hold values from 0 to 15, as said below
- pivot_inv: float32 [32, 8, 128, 128], P(('group', 'strip')), may hold values from -0.2 to 1
- lower_block: float32 [32, 7, 128, 128], P(('group', 'strip')), may hold values from -0.109375 to 0.109375
- upper_block: float32 [32, 7, 128, 128], P(('group', 'strip')), may hold values from -0.109375 to 0.109375
Outputs:
- vorticity: float32 [64, 128, 128], P(('group', 'strip'))
- displacement: float32 [32, 16, 1024], P(('group', 'strip'))
Inputs may be any that keep to these rules, and one draw needn't show every extreme that they name: `strip_riser`: in each aligned block of 2 strips (the strips of one device) no riser is named more than 2 times, and some block names one riser exactly 2 times. `riser_owner`: the 4 owners in a row are distinct devices.
All inputs are finite; a program needn't handle non-finite values.
Results may differ from a plain program's by a relative error of at most 0.0003.
Values sent between devices are 32-bit elements; how exact they have to be, the bound alone decides.
No kernel may reach another device: no remote copies, remote signals or barrier semaphores. Data moves between devices by JAX's collectives and lax.ppermute only.
A program may use at most 64 MiB of HBM per device.

v0:
```python
import jax
import jax.numpy as jnp
from jax import lax
from jax.sharding import PartitionSpec as P

NSUB = 8
COUPLED = 2
TIME_STEP = 0.25
VISCOSITY = 0.05
COUPLING = 0.5
EXACT_DOT = lax.Precision.HIGHEST


def make_kernels(grid_cells):
    centre = jnp.arange(grid_cells, dtype=jnp.float32) - grid_cells / 2.0 + 0.5
    near_x = (centre / (grid_cells / 16.0))[None, :]
    near_y = (centre / (grid_cells / 16.0))[:, None]
    bell_near = jnp.exp(-(near_x * near_x + near_y * near_y) / 2.0)
    source_x = -near_x * bell_near
    source_y = -near_y * bell_near
    wide_x = (centre / (grid_cells / 8.0))[None, :]
    wide_y = (centre / (grid_cells / 8.0))[:, None]
    bell_wide = jnp.exp(-(wide_x * wide_x + wide_y * wide_y) / 2.0)
    lift_kernel = -wide_x * bell_wide
    drag_kernel = wide_y * bell_wide
    lift_kernel = lift_kernel / jnp.sqrt(jnp.sum(lift_kernel * lift_kernel))
    drag_kernel = drag_kernel / jnp.sqrt(jnp.sum(drag_kernel * drag_kernel))
    return (source_x, source_y, lift_kernel, drag_kernel)


def strip_step(vorticity, flow_x, flow_y, motion, kernels, substeps):
    source_x, source_y, lift_kernel, drag_kernel = kernels
    halves = motion.reshape(motion.shape[0], 2, substeps)
    earlier = jnp.concatenate([jnp.zeros_like(halves[:, :, :1]), halves[:, :, :-1]], axis=2)
    velocity = halves - earlier
    lift_rows = []
    drag_rows = []
    for substep in range(substeps):
        right_cell = jnp.roll(vorticity, -1, axis=2)
        left_cell = jnp.roll(vorticity, 1, axis=2)
        upper_cell = jnp.roll(vorticity, -1, axis=1)
        lower_cell = jnp.roll(vorticity, 1, axis=1)
        laplacian = right_cell + left_cell + upper_cell + lower_cell - 4.0 * vorticity
        tendency = (
            VISCOSITY * laplacian
            - flow_x * (0.5 * (right_cell - left_cell))
            - flow_y * (0.5 * (upper_cell - lower_cell))
        )
        forcing = (
            velocity[:, 0, substep][:, None, None] * source_x
            - velocity[:, 1, substep][:, None, None] * source_y
        )
        vorticity = vorticity + TIME_STEP * tendency + COUPLING * forcing
        lift_rows.append(jnp.sum(vorticity * lift_kernel, axis=(1, 2)))
        drag_rows.append(jnp.sum(vorticity * drag_kernel, axis=(1, 2)))
    return (vorticity, jnp.stack(lift_rows + drag_rows, axis=1))


def apply_block(vectors, matrix):
    return lax.dot_general(vectors, matrix, (((1,), (1,)), ((), ())), precision=EXACT_DOT)


def first_contract(left_side, right_side):
    return lax.dot_general(left_side, right_side, (((0,), (0,)), ((), ())), precision=EXACT_DOT)


def beam_solve(beam_load, pivot_inv, lower_block, upper_block):
    block_count = pivot_inv.shape[0]
    block_size = pivot_inv.shape[1]
    blocks = beam_load.reshape(beam_load.shape[0], block_count, block_size)
    carried = [blocks[:, 0]]
    for block_index in range(1, block_count):
        pivoted = apply_block(carried[-1], pivot_inv[block_index - 1])
        carried.append(blocks[:, block_index] - apply_block(pivoted, lower_block[block_index - 1]))
    solved = [apply_block(carried[-1], pivot_inv[block_count - 1])]
    for block_index in range(block_count - 2, -1, -1):
        remainder = carried[block_index] - apply_block(solved[0], upper_block[block_index])
        solved.insert(0, apply_block(remainder, pivot_inv[block_index]))
    return jnp.concatenate(solved, axis=1)


def local(strip_fields, strip_riser, strip_node, riser_owner, pivot_inv, lower_block, upper_block):
    devices = lax.axis_size("strip")
    position = lax.axis_index("strip")
    per_device = strip_fields.shape[1]
    grid_cells = strip_fields.shape[2]
    node_count = pivot_inv.shape[1] * pivot_inv.shape[2]
    riser_count = riser_owner.shape[1]
    substeps = NSUB
    total_strips = per_device * devices * lax.axis_size("group")
    kernels = make_kernels(grid_cells)
    riser_match = (
        strip_riser[:, 0][:, None] == jnp.arange(riser_count, dtype=jnp.int32)[None, :]
    ).astype(jnp.int32)
    owner_index = jnp.sum(riser_match * riser_owner[0][None, :], axis=1)
    owned_here = owner_index == position
    node_hit = (
        owned_here[:, None]
        & (strip_node[:, None] == jnp.arange(node_count, dtype=jnp.int32)[None, :])
    ).astype(jnp.float32)
    local_owner = lax.dynamic_slice_in_dim(owner_index, position * per_device, per_device)
    local_node = lax.dynamic_slice_in_dim(strip_node, position * per_device, per_device)
    top_taper = 1.0 - jnp.arange(node_count, dtype=jnp.float32) / node_count
    vorticity = strip_fields[0]
    flow_x = strip_fields[1]
    flow_y = strip_fields[2]
    motion = jnp.zeros((per_device, 2 * substeps), jnp.float32)
    displacement = jnp.zeros((2 * substeps, node_count), jnp.float32)
    for coupled_step in range(COUPLED):
        vorticity, force_rows = strip_step(vorticity, flow_x, flow_y, motion, kernels, substeps)
        partial_drag = jnp.sum(force_rows[:, substeps:], axis=0)
        total_drag = lax.psum(partial_drag, ("group", "strip"))
        offset = total_drag / jnp.sqrt(jnp.float32(total_strips))
        beam_load = first_contract(
            lax.all_gather(force_rows, "strip", axis=0, tiled=True), node_hit
        )
        displacement = beam_solve(beam_load, pivot_inv[0], lower_block[0], upper_block[0])
        displacement = displacement.at[substeps:, :].add(offset[:, None] * top_taper[None, :])
        if coupled_step + 1 < COUPLED:
            every_owner = lax.all_gather(displacement[None], "strip", axis=0, tiled=True)
            chosen = jnp.take(every_owner, local_owner, axis=0)
            node_pick = jnp.broadcast_to(local_node[:, None, None], (per_device, 2 * substeps, 1))
            motion = jnp.take_along_axis(chosen, node_pick, axis=2)[:, :, 0]
    return (vorticity, displacement[None])


def solution(mesh):
    in_specs = (
        P(None, ("group", "strip"), None, None),
        P("group", None),
        P("group"),
        P("group", None),
        P(("group", "strip"), None, None, None),
        P(("group", "strip"), None, None, None),
        P(("group", "strip"), None, None, None),
    )
    out_specs = (P(("group", "strip"), None, None), P(("group", "strip"), None, None))
    return jax.shard_map(local, mesh=mesh, in_specs=in_specs, out_specs=out_specs, check_vma=False)
```

profile of v0, /device:TPU:0, one launch (start us, length us, event | category | flops | bytes accessed | tf_op | source)
XLA Modules:
  0.0 231.5 jit_solution(9136430588047142506)
XLA Ops:
  7.2 0.9 slice_bitcast_fusion
  8.5 0.8 copy-done
  12.4 0.7 multiply_reduce_fusion.32
  14.6 0.5 multiply_reduce_fusion.23
  15.9 42.0 %psum.14 = f32[8]{0:T(128)S(1)} all-reduce(f32[8]{0:T(128)S(1)} %reduce_sum.352), channel_id=1, replica_groups=mesh['group'=2,'strip'=16] {'group','strip'}, use_global_device_ids=true, to_apply=%region_20.21 | all-reduce | flops 8 | bytes 64 | tf_op jit(solution)/shard_map/psum | solution.py:112
  58.8 21.0 %all-gather = f32[16,2,16]{2,1,0:T(2,128)S(1)} all-gather(f32[1,2,16]{2,1,0:T(2,128)S(1)} %bitcast.564), channel_id=1, replica_groups=mesh['group'=2,'strip'=16] {'strip'}, dimensions={0}, use_global_device_ids=true | all-gather | bytes 2176 | tf_op jit(solution)/shard_map/all_gather | solution.py:115
  79.8 0.7 copy-done.6
  80.5 0.7 copy-done.5
  81.5 1.0 fusion.167
  82.5 1.1 convolution_subtract_fusion.27
  83.6 1.1 fusion.159
  84.7 1.1 convolution_subtract_fusion.26
  85.8 1.1 fusion.149
  86.9 1.1 convolution_subtract_fusion.25
  88.0 1.1 fusion.139
  89.0 1.1 convolution_subtract_fusion.24
  90.1 1.1 fusion.129
  91.2 1.1 convolution_subtract_fusion.23
  92.2 1.1 fusion.119
  93.3 1.1 convolution_subtract_fusion.22
  94.3 1.1 fusion.109
  95.4 1.1 convolution_subtract_fusion.21
  96.5 1.1 fusion.99
  99.3 0.3 convolution_subtract_fusion.16
  100.2 0.3 convolution_subtract_fusion.14
  100.9 0.6 copy-done.3
  102.2 33.8 %all-gather.4.cloned.1.call-done = f32[16,16,1024]{2,1,0:T(8,128)} async-done(((f32[1,16,1024]{2,1,0:T(8,128)}), f32[16,16,1024]{2,1,0:T(8,128)}) %all-gather.4.cloned.1.call-update) | async-done | bytes 1048592 | tf_op jit(solution)/shard_map/all_gather | solution.py:120
  136.0 1.8 gather_fusion
  137.8 0.8 gather_fusion.1
  142.2 1.1 multiply_reduce_fusion.7
  144.2 38.9 %psum.15 = f32[8]{0:T(128)S(1)} all-reduce(f32[8]{0:T(128)S(1)} %reduce_sum.369), channel_id=1, replica_groups=mesh['group'=2,'strip'=16] {'group','strip'}, use_global_device_ids=true, to_apply=%region_38.39 | all-reduce | flops 8 | bytes 64 | tf_op jit(solution)/shard_map/psum | solution.py:112
  183.9 20.6 %all-gather.1 = f32[16,2,16]{2,1,0:T(2,128)S(1)} all-gather(f32[1,2,16]{2,1,0:T(2,128)S(1)} %bitcast.565), channel_id=1, replica_groups=mesh['group'=2,'strip'=16] {'strip'}, dimensions={0}, use_global_device_ids=true | all-gather | bytes 2176 | tf_op jit(solution)/shard_map/all_gather | solution.py:115
  204.8 1.0 fusion.164
  205.8 1.1 convolution_subtract_fusion.13
  206.9 1.1 fusion.155
  208.0 1.1 convolution_subtract_fusion.12
  209.0 1.1 fusion.145
  210.1 1.1 convolution_subtract_fusion.11
  211.2 1.1 fusion.135
  212.2 1.1 convolution_subtract_fusion.10
  213.3 1.1 fusion.125
  214.3 1.1 convolution_subtract_fusion.9
  215.4 1.1 fusion.115
  216.5 1.1 convolution_subtract_fusion.8
  217.5 1.1 fusion.105
  218.6 1.1 convolution_subtract_fusion.7
  219.6 1.1 fusion.97
  224.1 0.6 copy-done.4
  (204 shorter events, 17.4 us)
Async XLA Ops:
  7.2 128.8 %all-gather.4.cloned.1.call-start = ((), (), s32[]{:S(2)}) async-start(), calls=%async_computation | async-start | bytes 1114112 | tf_op jit(solution)/shard_map/all_gather | solution.py:120
  8.3 1.0 copy-start
  79.8 0.7 copy-start.6
  79.8 0.7 copy-start.7
  80.5 0.7 copy-start.5
  84.7 12.9 %copy-start.2 = (f32[1,7,128,128]{3,2,1,0:T(8,128)S(1)}, f32[1,7,128,128]{3,2,1,0:T(8,128)}, u32[]{:S(2)}) copy-start(f32[1,7,128,128]{3,2,1,0:T(8,128)} %param.17) | copy-start | bytes 1376260
  85.8 12.0 %copy-start.1 = (f32[1,8,128,128]{3,2,1,0:T(8,128)S(1)}, f32[1,8,128,128]{3,2,1,0:T(8,128)}, u32[]{:S(2)}) copy-start(f32[1,8,128,128]{3,2,1,0:T(8,128)} %param.15) | copy-start | bytes 1572868
  100.9 0.6 copy-start.3
  224.1 0.6 copy-start.4
Sparse Core Ops, SparseCore 0:
  101.7 34.2 all-gather.3
where the time goes:
time: 233 us; the launch traced here: 232 us
  blocking collectives  123 us (53%)
  matrix products  38.5 us (17%)
  waiting for transfers between devices  33.8 us (15%)
  between operations  16.3 us (7%)
  local copies, waits for them, and re-layouts  14.4 us (6%)
  other arithmetic  5.94 us (3%)
    psum x2, blocking collectives, local(): total_drag = lax.psum(partial_drag, ('group', 'strip'))  80.9 us
    all_gather x2, blocking collectives, local(): lax.all_gather(force_rows, 'strip', axis=0, tiled=True)  41.6 us
    dot_general x58, matrix products, apply_block(): lax.dot_general(vectors, matrix, (((1,), (1,)), ((), ())), precision=EXAC...  38 us
    all_gather x1, waiting for transfers between devices, local(): lax.all_gather(displacement[None], 'strip', axis=0, tiled=True)  33.8 us
  transfers between devices with their start and end apart: 1, of which 1 were waited for; matrix products, arithmetic and copies ran while one was open for 0% of the time, Pallas kernels for 0%

commit v1 on v0

--- a/solution.py
+++ b/solution.py
@@ -9,6 +9,27 @@
 VISCOSITY = 0.05
 COUPLING = 0.5
 EXACT_DOT = lax.Precision.HIGHEST
+
+
+def unite_stocks(values, axis_key):
+    val, y, aux = (lax.psum(1, axis_name=axis_key), lax.axis_index(axis_key), values.shape[0])
+    vals = [(dev_i, (dev_i + 1) % val) for dev_i in range(val)]
+    samples = [(dev_i, (dev_i - 1) % val) for dev_i in range(val)]
+    right_arr = jnp.zeros((*values.shape[:0], val * aux, *values.shape[1:]), values.dtype)
+    right_arr = lax.dynamic_update_slice_in_dim(right_arr, values, y * aux, axis=0)
+    side_arr = e_now = values
+    before = val // 2
+    for k in range(1, before + 1):
+        side_arr = lax.ppermute(side_arr, axis_key, vals)
+        right_arr = lax.dynamic_update_slice_in_dim(
+            right_arr, side_arr, (y - k) % val * aux, axis=0
+        )
+        if k < val - before:
+            e_now = lax.ppermute(e_now, axis_key, samples)
+            right_arr = lax.dynamic_update_slice_in_dim(
+                right_arr, e_now, (y + k) % val * aux, axis=0
+            )
+    return right_arr
 
 
 def make_kernels(grid_cells):
@@ -111,9 +132,7 @@
         partial_drag = jnp.sum(force_rows[:, substeps:], axis=0)
         total_drag = lax.psum(partial_drag, ("group", "strip"))
         offset = total_drag / jnp.sqrt(jnp.float32(total_strips))
-        beam_load = first_contract(
-            lax.all_gather(force_rows, "strip", axis=0, tiled=True), node_hit
-        )
+        beam_load = first_contract(unite_stocks(force_rows, "strip"), node_hit)
         displacement = beam_solve(beam_load, pivot_inv[0], lower_block[0], upper_block[0])
         displacement = displacement.at[substeps:, :].add(offset[:, None] * top_taper[None, :])
         if coupled_step + 1 < COUPLED:

time: 233 us -> 277 us (1.19)
  starting transfers between devices: 0.04 us -> 63 us
  blocking collectives: 123 us -> 75.1 us
  waiting for transfers between devices: 33.8 us -> 62.2 us
    ppermute x0 -> x30, starting transfers between devices: none -> 63 us  [the longest x14 62 us: unite_stocks(): e_now = lax.ppermute(e_now, axis_key, samples)]
    all_gather x2 -> x0, blocking collectives: 41.6 us -> none  [local(): lax.all_gather(force_rows, 'strip', axis=0, tiled=True)]
    ppermute x0 -> x30, waiting for transfers between devices: none -> 26.6 us  [the longest x16 26 us: unite_stocks(): side_arr = lax.ppermute(side_arr, axis_key, vals)]
    psum x2, blocking collectives: 80.9 us -> 75.1 us  [local(): total_drag = lax.psum(partial_drag, ('group', 'strip'))]
  transfers between devices with their start and end apart: 1 -> 31, of which waited for: 1 -> 26; matrix products, arithmetic and copies ran while one was open for 0% -> 0% of each run, Pallas kernels for 0% -> 0%
where the time goes in v1:
time: 277 us; the launch traced here: 275 us
  blocking collectives  75.1 us (27%)
  starting transfers between devices  63 us (23%)
  waiting for transfers between devices  62.2 us (22%)
  matrix products  38.5 us (14%)
  between operations  16.7 us (6%)
  local copies, waits for them, and re-layouts  14 us (5%)
  other arithmetic  5.84 us (2%)
    psum x2, blocking collectives, local(): total_drag = lax.psum(partial_drag, ('group', 'strip'))  75.1 us
    ppermute x14, starting transfers between devices, unite_stocks(): e_now = lax.ppermute(e_now, axis_key, samples)  62 us
    dot_general x58, matrix products, apply_block(): lax.dot_general(vectors, matrix, (((1,), (1,)), ((), ())), precision=EXAC...  38.1 us
    all_gather x1, waiting for transfers between devices, local(): lax.all_gather(displacement[None], 'strip', axis=0, tiled=True)  35.5 us
    ppermute x16, waiting for transfers between devices, unite_stocks(): side_arr = lax.ppermute(side_arr, axis_key, vals)  26 us
  transfers between devices with their start and end apart: 31, of which 26 were waited for; matrix products, arithmetic and copies ran while one was open for 0% of the time, Pallas kernels for 0%

profile of v1, /device:TPU:0, one launch (start us, length us, event | category | flops | bytes accessed | tf_op | source)
XLA Modules:
  0.0 275.3 jit_solution(8888911598040440307)
XLA Ops:
  17.1 5.1 %collective-permute-start.1 = (f32[2,16]{1,0:T(2,128)S(1)}, f32[2,16]{1,0:T(2,128)S(1)}, u32[]{:S(2)}, u32[]{:S(2)}) collective-permute-start(f32[2,16]{1,0:T(2,128)S(1)} %stack.122), channel_id=1, source_target_pairs={{0,15},{1,0},{2,1},{3,2},{4,3},{5,4},{6,5},{7,6},{8,7},{9,8},{10,9... | collective-permute-start | bytes 392 | tf_op jit(solution)/shard_map/ppermute | solution.py:28
  22.5 38.3 %psum.14 = f32[8]{0:T(128)S(1)} all-reduce(f32[8]{0:T(128)S(1)} %reduce_sum.352), channel_id=1, replica_groups=mesh['group'=2,'strip'=16] {'group','strip'}, use_global_device_ids=true, to_apply=%region_20.21 | all-reduce | flops 8 | bytes 64 | tf_op jit(solution)/shard_map/psum | solution.py:133
  61.7 4.4 %collective-permute-start.3 = (f32[2,16]{1,0:T(2,128)S(1)}, f32[2,16]{1,0:T(2,128)S(1)}, u32[]{:S(2)}, u32[]{:S(2)}) collective-permute-start(f32[2,16]{1,0:T(2,128)S(1)} %collective-permute-done.1), channel_id=1, source_target_pairs={{0,15},{1,0},{2,1},{3,2},{4,3},{5,4},{6,5},{7,6},{8,7},{9,8},{10,9... | collective-permute-start | bytes 392 | tf_op jit(solution)/shard_map/ppermute | solution.py:28
  66.1 1.2 collective-permute-done.2
  67.4 4.4 %collective-permute-start.5 = (f32[2,16]{1,0:T(2,128)S(1)}, f32[2,16]{1,0:T(2,128)S(1)}, u32[]{:S(2)}, u32[]{:S(2)}) collective-permute-start(f32[2,16]{1,0:T(2,128)S(1)} %collective-permute-done.3), channel_id=1, source_target_pairs={{0,15},{1,0},{2,1},{3,2},{4,3},{5,4},{6,5},{7,6},{8,7},{9,8},{10,9... | collective-permute-start | bytes 392 | tf_op jit(solution)/shard_map/ppermute | solution.py:28
  71.8 1.2 collective-permute-done.4
  73.1 4.4 %collective-permute-start.7 = (f32[2,16]{1,0:T(2,128)S(1)}, f32[2,16]{1,0:T(2,128)S(1)}, u32[]{:S(2)}, u32[]{:S(2)}) collective-permute-start(f32[2,16]{1,0:T(2,128)S(1)} %collective-permute-done.5), channel_id=1, source_target_pairs={{0,15},{1,0},{2,1},{3,2},{4,3},{5,4},{6,5},{7,6},{8,7},{9,8},{10,9... | collective-permute-start | bytes 392 | tf_op jit(solution)/shard_map/ppermute | solution.py:28
  77.5 1.2 collective-permute-done.6
  78.8 4.4 %collective-permute-start.9 = (f32[2,16]{1,0:T(2,128)S(1)}, f32[2,16]{1,0:T(2,128)S(1)}, u32[]{:S(2)}, u32[]{:S(2)}) collective-permute-start(f32[2,16]{1,0:T(2,128)S(1)} %collective-permute-done.7), channel_id=1, source_target_pairs={{0,15},{1,0},{2,1},{3,2},{4,3},{5,4},{6,5},{7,6},{8,7},{9,8},{10,9... | collective-permute-start | bytes 392 | tf_op jit(solution)/shard_map/ppermute | solution.py:28
  83.2 1.2 collective-permute-done.8
  84.5 4.4 %collective-permute-start.11 = (f32[2,16]{1,0:T(2,128)S(1)}, f32[2,16]{1,0:T(2,128)S(1)}, u32[]{:S(2)}, u32[]{:S(2)}) collective-permute-start(f32[2,16]{1,0:T(2,128)S(1)} %collective-permute-done.9), channel_id=1, source_target_pairs={{0,15},{1,0},{2,1},{3,2},{4,3},{5,4},{6,5},{7,6},{8,7},{9,8},{10,9... | collective-permute-start | bytes 392 | tf_op jit(solution)/shard_map/ppermute | solution.py:28
  88.9 1.2 collective-permute-done.10
  90.2 4.4 %collective-permute-start.13 = (f32[2,16]{1,0:T(2,128)S(1)}, f32[2,16]{1,0:T(2,128)S(1)}, u32[]{:S(2)}, u32[]{:S(2)}) collective-permute-start(f32[2,16]{1,0:T(2,128)S(1)} %collective-permute-done.11), channel_id=1, source_target_pairs={{0,15},{1,0},{2,1},{3,2},{4,3},{5,4},{6,5},{7,6},{8,7},{9,8},{10,9... | collective-permute-start | bytes 392 | tf_op jit(solution)/shard_map/ppermute | solution.py:28
  94.6 1.2 collective-permute-done.12
  95.9 5.6 %collective-permute-done.14 = f32[2,16]{1,0:T(2,128)S(1)} collective-permute-done((f32[2,16]{1,0:T(2,128)S(1)}, f32[2,16]{1,0:T(2,128)S(1)}, u32[]{:S(2)}, u32[]{:S(2)}) %collective-permute-start.14) | collective-permute-done | bytes 160 | tf_op jit(solution)/shard_map/ppermute | solution.py:23
  102.9 1.1 convolution_subtract_fusion.27
  105.0 1.1 convolution_subtract_fusion.26
  106.2 1.1 fusion.149
  107.2 1.1 convolution_subtract_fusion.25
  109.4 1.1 convolution_subtract_fusion.24
  111.5 1.1 convolution_subtract_fusion.23
  113.6 1.1 convolution_subtract_fusion.22
  115.7 1.1 convolution_subtract_fusion.21
  122.5 35.5 %all-gather.2.cloned.1.call-done = f32[16,16,1024]{2,1,0:T(8,128)} async-done(((f32[1,16,1024]{2,1,0:T(8,128)}), f32[16,16,1024]{2,1,0:T(8,128)}) %all-gather.2.cloned.1.call-update) | async-done | bytes 1048592 | tf_op jit(solution)/shard_map/all_gather | solution.py:139
  158.0 1.8 gather_fusion
  164.2 1.1 multiply_reduce_fusion.7
  167.3 4.2 %collective-permute-start.16 = (f32[2,16]{1,0:T(2,128)S(1)}, f32[2,16]{1,0:T(2,128)S(1)}, u32[]{:S(2)}, u32[]{:S(2)}) collective-permute-start(f32[2,16]{1,0:T(2,128)S(1)} %stack.140), channel_id=1, source_target_pairs={{0,15},{1,0},{2,1},{3,2},{4,3},{5,4},{6,5},{7,6},{8,7},{9,8},{10,9... | collective-permute-start | bytes 392 | tf_op jit(solution)/shard_map/ppermute | solution.py:28
  171.5 36.8 %psum.15 = f32[8]{0:T(128)S(1)} all-reduce(f32[8]{0:T(128)S(1)} %reduce_sum.369), channel_id=1, replica_groups=mesh['group'=2,'strip'=16] {'group','strip'}, use_global_device_ids=true, to_apply=%region_38.39 | all-reduce | flops 8 | bytes 64 | tf_op jit(solution)/shard_map/psum | solution.py:133
  208.5 4.4 %collective-permute-start.18 = (f32[2,16]{1,0:T(2,128)S(1)}, f32[2,16]{1,0:T(2,128)S(1)}, u32[]{:S(2)}, u32[]{:S(2)}) collective-permute-start(f32[2,16]{1,0:T(2,128)S(1)} %collective-permute-done.16), channel_id=1, source_target_pairs={{0,15},{1,0},{2,1},{3,2},{4,3},{5,4},{6,5},{7,6},{8,7},{9,8},{10,9... | collective-permute-start | bytes 392 | tf_op jit(solution)/shard_map/ppermute | solution.py:28
  212.9 1.2 collective-permute-done.17
  214.2 4.4 %collective-permute-start.20 = (f32[2,16]{1,0:T(2,128)S(1)}, f32[2,16]{1,0:T(2,128)S(1)}, u32[]{:S(2)}, u32[]{:S(2)}) collective-permute-start(f32[2,16]{1,0:T(2,128)S(1)} %collective-permute-done.18), channel_id=1, source_target_pairs={{0,15},{1,0},{2,1},{3,2},{4,3},{5,4},{6,5},{7,6},{8,7},{9,8},{10,9... | collective-permute-start | bytes 392 | tf_op jit(solution)/shard_map/ppermute | solution.py:28
  218.6 1.2 collective-permute-done.19
  219.9 4.4 %collective-permute-start.22 = (f32[2,16]{1,0:T(2,128)S(1)}, f32[2,16]{1,0:T(2,128)S(1)}, u32[]{:S(2)}, u32[]{:S(2)}) collective-permute-start(f32[2,16]{1,0:T(2,128)S(1)} %collective-permute-done.20), channel_id=1, source_target_pairs={{0,15},{1,0},{2,1},{3,2},{4,3},{5,4},{6,5},{7,6},{8,7},{9,8},{10,9... | collective-permute-start | bytes 392 | tf_op jit(solution)/shard_map/ppermute | solution.py:28
  224.3 1.2 collective-permute-done.21
  225.6 4.4 %collective-permute-start.24 = (f32[2,16]{1,0:T(2,128)S(1)}, f32[2,16]{1,0:T(2,128)S(1)}, u32[]{:S(2)}, u32[]{:S(2)}) collective-permute-start(f32[2,16]{1,0:T(2,128)S(1)} %collective-permute-done.22), channel_id=1, source_target_pairs={{0,15},{1,0},{2,1},{3,2},{4,3},{5,4},{6,5},{7,6},{8,7},{9,8},{10,9... | collective-permute-start | bytes 392 | tf_op jit(solution)/shard_map/ppermute | solution.py:28
  230.0 1.2 collective-permute-done.23
  231.3 4.4 %collective-permute-start.26 = (f32[2,16]{1,0:T(2,128)S(1)}, f32[2,16]{1,0:T(2,128)S(1)}, u32[]{:S(2)}, u32[]{:S(2)}) collective-permute-start(f32[2,16]{1,0:T(2,128)S(1)} %collective-permute-done.24), channel_id=1, source_target_pairs={{0,15},{1,0},{2,1},{3,2},{4,3},{5,4},{6,5},{7,6},{8,7},{9,8},{10,9... | collective-permute-start | bytes 392 | tf_op jit(solution)/shard_map/ppermute | solution.py:28
  235.7 1.2 collective-permute-done.25
  236.9 4.4 %collective-permute-start.28 = (f32[2,16]{1,0:T(2,128)S(1)}, f32[2,16]{1,0:T(2,128)S(1)}, u32[]{:S(2)}, u32[]{:S(2)}) collective-permute-start(f32[2,16]{1,0:T(2,128)S(1)} %collective-permute-done.26), channel_id=1, source_target_pairs={{0,15},{1,0},{2,1},{3,2},{4,3},{5,4},{6,5},{7,6},{8,7},{9,8},{10,9... | collective-permute-start | bytes 392 | tf_op jit(solution)/shard_map/ppermute | solution.py:28
  241.3 1.2 collective-permute-done.27
  242.6 5.6 %collective-permute-done.29 = f32[2,16]{1,0:T(2,128)S(1)} collective-permute-done((f32[2,16]{1,0:T(2,128)S(1)}, f32[2,16]{1,0:T(2,128)S(1)}, u32[]{:S(2)}, u32[]{:S(2)}) %collective-permute-start.29) | collective-permute-done | bytes 160 | tf_op jit(solution)/shard_map/ppermute | solution.py:23
  249.6 1.1 convolution_subtract_fusion.13
  251.7 1.1 convolution_subtract_fusion.12
  253.9 1.1 convolution_subtract_fusion.11
  256.0 1.1 convolution_subtract_fusion.10
  258.1 1.1 convolution_subtract_fusion.9
  260.2 1.1 convolution_subtract_fusion.8
  262.4 1.1 convolution_subtract_fusion.7
  (296 shorter events, 41.1 us)
Async XLA Ops:
  7.2 150.8 %all-gather.2.cloned.1.call-start = ((), (), s32[]{:S(2)}) async-start(), calls=%async_computation | async-start | bytes 1114112 | tf_op jit(solution)/shard_map/all_gather | solution.py:139
  8.3 1.0 copy-start
  16.6 45.0 %collective-permute-start = (f32[2,16]{1,0:T(2,128)S(1)}, f32[2,16]{1,0:T(2,128)S(1)}, u32[]{:S(2)}, u32[]{:S(2)}) collective-permute-start(f32[2,16]{1,0:T(2,128)S(1)} %stack.122), channel_id=1, source_target_pairs={{0,1},{1,2},{2,3},{3,4},{4,5},{5,6},{6,7},{7,8},{8,9},{9,10},{10,1... | collective-permute-start | bytes 392 | tf_op jit(solution)/shard_map/ppermute | solution.py:23
  17.1 44.6 %collective-permute-start.1 = (f32[2,16]{1,0:T(2,128)S(1)}, f32[2,16]{1,0:T(2,128)S(1)}, u32[]{:S(2)}, u32[]{:S(2)}) collective-permute-start(f32[2,16]{1,0:T(2,128)S(1)} %stack.122), channel_id=1, source_target_pairs={{0,15},{1,0},{2,1},{3,2},{4,3},{5,4},{6,5},{7,6},{8,7},{9,8},{10,9... | collective-permute-start | bytes 392 | tf_op jit(solution)/shard_map/ppermute | solution.py:28
  60.7 0.7 copy-start.6
  60.7 0.7 copy-start.7
  61.6 5.7 %collective-permute-start.2 = (f32[2,16]{1,0:T(2,128)S(1)}, f32[2,16]{1,0:T(2,128)S(1)}, u32[]{:S(2)}, u32[]{:S(2)}) collective-permute-start(f32[2,16]{1,0:T(2,128)S(1)} %collective-permute-done), channel_id=1, source_target_pairs={{0,1},{1,2},{2,3},{3,4},{4,5},{5,6},{6,7},{7,8},{8,9},{9,10},{10,1... | collective-permute-start | bytes 392 | tf_op jit(solution)/shard_map/ppermute | solution.py:23
  61.7 5.7 %collective-permute-start.3 = (f32[2,16]{1,0:T(2,128)S(1)}, f32[2,16]{1,0:T(2,128)S(1)}, u32[]{:S(2)}, u32[]{:S(2)}) collective-permute-start(f32[2,16]{1,0:T(2,128)S(1)} %collective-permute-done.1), channel_id=1, source_target_pairs={{0,15},{1,0},{2,1},{3,2},{4,3},{5,4},{6,5},{7,6},{8,7},{9,8},{10,9... | collective-permute-start | bytes 392 | tf_op jit(solution)/shard_map/ppermute | solution.py:28
  67.4 5.7 %collective-permute-start.4 = (f32[2,16]{1,0:T(2,128)S(1)}, f32[2,16]{1,0:T(2,128)S(1)}, u32[]{:S(2)}, u32[]{:S(2)}) collective-permute-start(f32[2,16]{1,0:T(2,128)S(1)} %collective-permute-done.2), channel_id=1, source_target_pairs={{0,1},{1,2},{2,3},{3,4},{4,5},{5,6},{6,7},{7,8},{8,9},{9,10},{10,1... | collective-permute-start | bytes 392 | tf_op jit(solution)/shard_map/ppermute | solution.py:23
  67.4 5.7 %collective-permute-start.5 = (f32[2,16]{1,0:T(2,128)S(1)}, f32[2,16]{1,0:T(2,128)S(1)}, u32[]{:S(2)}, u32[]{:S(2)}) collective-permute-start(f32[2,16]{1,0:T(2,128)S(1)} %collective-permute-done.3), channel_id=1, source_target_pairs={{0,15},{1,0},{2,1},{3,2},{4,3},{5,4},{6,5},{7,6},{8,7},{9,8},{10,9... | collective-permute-start | bytes 392 | tf_op jit(solution)/shard_map/ppermute | solution.py:28
  73.1 5.7 %collective-permute-start.6 = (f32[2,16]{1,0:T(2,128)S(1)}, f32[2,16]{1,0:T(2,128)S(1)}, u32[]{:S(2)}, u32[]{:S(2)}) collective-permute-start(f32[2,16]{1,0:T(2,128)S(1)} %collective-permute-done.4), channel_id=1, source_target_pairs={{0,1},{1,2},{2,3},{3,4},{4,5},{5,6},{6,7},{7,8},{8,9},{9,10},{10,1... | collective-permute-start | bytes 392 | tf_op jit(solution)/shard_map/ppermute | solution.py:23
  73.1 5.7 %collective-permute-start.7 = (f32[2,16]{1,0:T(2,128)S(1)}, f32[2,16]{1,0:T(2,128)S(1)}, u32[]{:S(2)}, u32[]{:S(2)}) collective-permute-start(f32[2,16]{1,0:T(2,128)S(1)} %collective-permute-done.5), channel_id=1, source_target_pairs={{0,15},{1,0},{2,1},{3,2},{4,3},{5,4},{6,5},{7,6},{8,7},{9,8},{10,9... | collective-permute-start | bytes 392 | tf_op jit(solution)/shard_map/ppermute | solution.py:28
  78.7 5.7 %collective-permute-start.8 = (f32[2,16]{1,0:T(2,128)S(1)}, f32[2,16]{1,0:T(2,128)S(1)}, u32[]{:S(2)}, u32[]{:S(2)}) collective-permute-start(f32[2,16]{1,0:T(2,128)S(1)} %collective-permute-done.6), channel_id=1, source_target_pairs={{0,1},{1,2},{2,3},{3,4},{4,5},{5,6},{6,7},{7,8},{8,9},{9,10},{10,1... | collective-permute-start | bytes 392 | tf_op jit(solution)/shard_map/ppermute | solution.py:23
  78.8 5.7 %collective-permute-start.9 = (f32[2,16]{1,0:T(2,128)S(1)}, f32[2,16]{1,0:T(2,128)S(1)}, u32[]{:S(2)}, u32[]{:S(2)}) collective-permute-start(f32[2,16]{1,0:T(2,128)S(1)} %collective-permute-done.7), channel_id=1, source_target_pairs={{0,15},{1,0},{2,1},{3,2},{4,3},{5,4},{6,5},{7,6},{8,7},{9,8},{10,9... | collective-permute-start | bytes 392 | tf_op jit(solution)/shard_map/ppermute | solution.py:28
  84.4 5.7 %collective-permute-start.10 = (f32[2,16]{1,0:T(2,128)S(1)}, f32[2,16]{1,0:T(2,128)S(1)}, u32[]{:S(2)}, u32[]{:S(2)}) collective-permute-start(f32[2,16]{1,0:T(2,128)S(1)} %collective-permute-done.8), channel_id=1, source_target_pairs={{0,1},{1,2},{2,3},{3,4},{4,5},{5,6},{6,7},{7,8},{8,9},{9,10},{10,1... | collective-permute-start | bytes 392 | tf_op jit(solution)/shard_map/ppermute | solution.py:23
  84.5 5.7 %collective-permute-start.11 = (f32[2,16]{1,0:T(2,128)S(1)}, f32[2,16]{1,0:T(2,128)S(1)}, u32[]{:S(2)}, u32[]{:S(2)}) collective-permute-start(f32[2,16]{1,0:T(2,128)S(1)} %collective-permute-done.9), channel_id=1, source_target_pairs={{0,15},{1,0},{2,1},{3,2},{4,3},{5,4},{6,5},{7,6},{8,7},{9,8},{10,9... | collective-permute-start | bytes 392 | tf_op jit(solution)/shard_map/ppermute | solution.py:28
  90.1 5.7 %collective-permute-start.12 = (f32[2,16]{1,0:T(2,128)S(1)}, f32[2,16]{1,0:T(2,128)S(1)}, u32[]{:S(2)}, u32[]{:S(2)}) collective-permute-start(f32[2,16]{1,0:T(2,128)S(1)} %collective-permute-done.10), channel_id=1, source_target_pairs={{0,1},{1,2},{2,3},{3,4},{4,5},{5,6},{6,7},{7,8},{8,9},{9,10},{10,1... | collective-permute-start | bytes 392 | tf_op jit(solution)/shard_map/ppermute | solution.py:23
  90.2 5.7 %collective-permute-start.13 = (f32[2,16]{1,0:T(2,128)S(1)}, f32[2,16]{1,0:T(2,128)S(1)}, u32[]{:S(2)}, u32[]{:S(2)}) collective-permute-start(f32[2,16]{1,0:T(2,128)S(1)} %collective-permute-done.11), channel_id=1, source_target_pairs={{0,15},{1,0},{2,1},{3,2},{4,3},{5,4},{6,5},{7,6},{8,7},{9,8},{10,9... | collective-permute-start | bytes 392 | tf_op jit(solution)/shard_map/ppermute | solution.py:28
  95.8 5.7 %collective-permute-start.14 = (f32[2,16]{1,0:T(2,128)S(1)}, f32[2,16]{1,0:T(2,128)S(1)}, u32[]{:S(2)}, u32[]{:S(2)}) collective-permute-start(f32[2,16]{1,0:T(2,128)S(1)} %collective-permute-done.12), channel_id=1, source_target_pairs={{0,1},{1,2},{2,3},{3,4},{4,5},{5,6},{6,7},{7,8},{8,9},{9,10},{10,1... | collective-permute-start | bytes 392 | tf_op jit(solution)/shard_map/ppermute | solution.py:23
  95.9 5.6 %copy-start.5 = (s32[32]{0:T(128)S(1)}, s32[32]{0:T(128)}, u32[]{:S(2)}) copy-start(s32[32]{0:T(128)} %param.13) | copy-start | bytes 388
  105.0 12.9 %copy-start.2 = (f32[1,7,128,128]{3,2,1,0:T(8,128)S(1)}, f32[1,7,128,128]{3,2,1,0:T(8,128)}, u32[]{:S(2)}) copy-start(f32[1,7,128,128]{3,2,1,0:T(8,128)} %param.17) | copy-start | bytes 1376260
  106.1 12.0 %copy-start.1 = (f32[1,8,128,128]{3,2,1,0:T(8,128)S(1)}, f32[1,8,128,128]{3,2,1,0:T(8,128)}, u32[]{:S(2)}) copy-start(f32[1,8,128,128]{3,2,1,0:T(8,128)} %param.15) | copy-start | bytes 1572868
  121.2 0.6 copy-start.3
  167.0 41.4 %collective-permute-start.15 = (f32[2,16]{1,0:T(2,128)S(1)}, f32[2,16]{1,0:T(2,128)S(1)}, u32[]{:S(2)}, u32[]{:S(2)}) collective-permute-start(f32[2,16]{1,0:T(2,128)S(1)} %stack.140), channel_id=1, source_target_pairs={{0,1},{1,2},{2,3},{3,4},{4,5},{5,6},{6,7},{7,8},{8,9},{9,10},{10,1... | collective-permute-start | bytes 392 | tf_op jit(solution)/shard_map/ppermute | solution.py:23
  167.3 41.2 %collective-permute-start.16 = (f32[2,16]{1,0:T(2,128)S(1)}, f32[2,16]{1,0:T(2,128)S(1)}, u32[]{:S(2)}, u32[]{:S(2)}) collective-permute-start(f32[2,16]{1,0:T(2,128)S(1)} %stack.140), channel_id=1, source_target_pairs={{0,15},{1,0},{2,1},{3,2},{4,3},{5,4},{6,5},{7,6},{8,7},{9,8},{10,9... | collective-permute-start | bytes 392 | tf_op jit(solution)/shard_map/ppermute | solution.py:28
  208.4 5.7 %collective-permute-start.17 = (f32[2,16]{1,0:T(2,128)S(1)}, f32[2,16]{1,0:T(2,128)S(1)}, u32[]{:S(2)}, u32[]{:S(2)}) collective-permute-start(f32[2,16]{1,0:T(2,128)S(1)} %collective-permute-done.15), channel_id=1, source_target_pairs={{0,1},{1,2},{2,3},{3,4},{4,5},{5,6},{6,7},{7,8},{8,9},{9,10},{10,1... | collective-permute-start | bytes 392 | tf_op jit(solution)/shard_map/ppermute | solution.py:23
  208.5 5.7 %collective-permute-start.18 = (f32[2,16]{1,0:T(2,128)S(1)}, f32[2,16]{1,0:T(2,128)S(1)}, u32[]{:S(2)}, u32[]{:S(2)}) collective-permute-start(f32[2,16]{1,0:T(2,128)S(1)} %collective-permute-done.16), channel_id=1, source_target_pairs={{0,15},{1,0},{2,1},{3,2},{4,3},{5,4},{6,5},{7,6},{8,7},{9,8},{10,9... | collective-permute-start | bytes 392 | tf_op jit(solution)/shard_map/ppermute | solution.py:28
  214.1 5.7 %collective-permute-start.19 = (f32[2,16]{1,0:T(2,128)S(1)}, f32[2,16]{1,0:T(2,128)S(1)}, u32[]{:S(2)}, u32[]{:S(2)}) collective-permute-start(f32[2,16]{1,0:T(2,128)S(1)} %collective-permute-done.17), channel_id=1, source_target_pairs={{0,1},{1,2},{2,3},{3,4},{4,5},{5,6},{6,7},{7,8},{8,9},{9,10},{10,1... | collective-permute-start | bytes 392 | tf_op jit(solution)/shard_map/ppermute | solution.py:23
  214.2 5.7 %collective-permute-start.20 = (f32[2,16]{1,0:T(2,128)S(1)}, f32[2,16]{1,0:T(2,128)S(1)}, u32[]{:S(2)}, u32[]{:S(2)}) collective-permute-start(f32[2,16]{1,0:T(2,128)S(1)} %collective-permute-done.18), channel_id=1, source_target_pairs={{0,15},{1,0},{2,1},{3,2},{4,3},{5,4},{6,5},{7,6},{8,7},{9,8},{10,9... | collective-permute-start | bytes 392 | tf_op jit(solution)/shard_map/ppermute | solution.py:28
  219.8 5.7 %collective-permute-start.21 = (f32[2,16]{1,0:T(2,128)S(1)}, f32[2,16]{1,0:T(2,128)S(1)}, u32[]{:S(2)}, u32[]{:S(2)}) collective-permute-start(f32[2,16]{1,0:T(2,128)S(1)} %collective-permute-done.19), channel_id=1, source_target_pairs={{0,1},{1,2},{2,3},{3,4},{4,5},{5,6},{6,7},{7,8},{8,9},{9,10},{10,1... | collective-permute-start | bytes 392 | tf_op jit(solution)/shard_map/ppermute | solution.py:23
  219.9 5.7 %collective-permute-start.22 = (f32[2,16]{1,0:T(2,128)S(1)}, f32[2,16]{1,0:T(2,128)S(1)}, u32[]{:S(2)}, u32[]{:S(2)}) collective-permute-start(f32[2,16]{1,0:T(2,128)S(1)} %collective-permute-done.20), channel_id=1, source_target_pairs={{0,15},{1,0},{2,1},{3,2},{4,3},{5,4},{6,5},{7,6},{8,7},{9,8},{10,9... | collective-permute-start | bytes 392 | tf_op jit(solution)/shard_map/ppermute | solution.py:28
  225.5 5.7 %collective-permute-start.23 = (f32[2,16]{1,0:T(2,128)S(1)}, f32[2,16]{1,0:T(2,128)S(1)}, u32[]{:S(2)}, u32[]{:S(2)}) collective-permute-start(f32[2,16]{1,0:T(2,128)S(1)} %collective-permute-done.21), channel_id=1, source_target_pairs={{0,1},{1,2},{2,3},{3,4},{4,5},{5,6},{6,7},{7,8},{8,9},{9,10},{10,1... | collective-permute-start | bytes 392 | tf_op jit(solution)/shard_map/ppermute | solution.py:23
  225.6 5.7 %collective-permute-start.24 = (f32[2,16]{1,0:T(2,128)S(1)}, f32[2,16]{1,0:T(2,128)S(1)}, u32[]{:S(2)}, u32[]{:S(2)}) collective-permute-start(f32[2,16]{1,0:T(2,128)S(1)} %collective-permute-done.22), channel_id=1, source_target_pairs={{0,15},{1,0},{2,1},{3,2},{4,3},{5,4},{6,5},{7,6},{8,7},{9,8},{10,9... | collective-permute-start | bytes 392 | tf_op jit(solution)/shard_map/ppermute | solution.py:28
  231.2 5.7 %collective-permute-start.25 = (f32[2,16]{1,0:T(2,128)S(1)}, f32[2,16]{1,0:T(2,128)S(1)}, u32[]{:S(2)}, u32[]{:S(2)}) collective-permute-start(f32[2,16]{1,0:T(2,128)S(1)} %collective-permute-done.23), channel_id=1, source_target_pairs={{0,1},{1,2},{2,3},{3,4},{4,5},{5,6},{6,7},{7,8},{8,9},{9,10},{10,1... | collective-permute-start | bytes 392 | tf_op jit(solution)/shard_map/ppermute | solution.py:23
  231.3 5.7 %collective-permute-start.26 = (f32[2,16]{1,0:T(2,128)S(1)}, f32[2,16]{1,0:T(2,128)S(1)}, u32[]{:S(2)}, u32[]{:S(2)}) collective-permute-start(f32[2,16]{1,0:T(2,128)S(1)} %collective-permute-done.24), channel_id=1, source_target_pairs={{0,15},{1,0},{2,1},{3,2},{4,3},{5,4},{6,5},{7,6},{8,7},{9,8},{10,9... | collective-permute-start | bytes 392 | tf_op jit(solution)/shard_map/ppermute | solution.py:28
  236.9 5.7 %collective-permute-start.27 = (f32[2,16]{1,0:T(2,128)S(1)}, f32[2,16]{1,0:T(2,128)S(1)}, u32[]{:S(2)}, u32[]{:S(2)}) collective-permute-start(f32[2,16]{1,0:T(2,128)S(1)} %collective-permute-done.25), channel_id=1, source_target_pairs={{0,1},{1,2},{2,3},{3,4},{4,5},{5,6},{6,7},{7,8},{8,9},{9,10},{10,1... | collective-permute-start | bytes 392 | tf_op jit(solution)/shard_map/ppermute | solution.py:23
  236.9 5.7 %collective-permute-start.28 = (f32[2,16]{1,0:T(2,128)S(1)}, f32[2,16]{1,0:T(2,128)S(1)}, u32[]{:S(2)}, u32[]{:S(2)}) collective-permute-start(f32[2,16]{1,0:T(2,128)S(1)} %collective-permute-done.26), channel_id=1, source_target_pairs={{0,15},{1,0},{2,1},{3,2},{4,3},{5,4},{6,5},{7,6},{8,7},{9,8},{10,9... | collective-permute-start | bytes 392 | tf_op jit(solution)/shard_map/ppermute | solution.py:28
  242.6 5.7 %collective-permute-start.29 = (f32[2,16]{1,0:T(2,128)S(1)}, f32[2,16]{1,0:T(2,128)S(1)}, u32[]{:S(2)}, u32[]{:S(2)}) collective-permute-start(f32[2,16]{1,0:T(2,128)S(1)} %collective-permute-done.27), channel_id=1, source_target_pairs={{0,1},{1,2},{2,3},{3,4},{4,5},{5,6},{6,7},{7,8},{8,9},{9,10},{10,1... | collective-permute-start | bytes 392 | tf_op jit(solution)/shard_map/ppermute | solution.py:23
  267.8 0.6 copy-start.4
Sparse Core Ops, SparseCore 0:
  122.0 35.9 all-gather.1
